TPU v7x, 32 devices: a whole 2x2x4 slice. The times are simulated.
32 devices in a mesh: groups: 2 (over x), blk: 16 (over z, y, core).
Axes of the slice: x: 2, y: 2, z: 4, core: 2. Of those that a mesh axis runs over, the one named last changes fastest.
Arguments:
- contacts: float32 [512, 6144], P(('groups', 'blk')), parts along dimension 0, may hold values from 0.1 to 10
- widths: int32 [12288], P('groups'), parts along dimension 0, may hold values from 0 to 3
- masked_bins: int32 [768], P('groups'), parts along dimension 0, may hold values from 0 to 6143, as said below
- row_start: int32 [2], P('groups'), parts along dimension 0, may hold values from 0 to 5888
Outputs:
- correlation: float32 [512, 256], P(('groups', 'blk')), parts along dimension 0
There are 2 independent parts, one for each index of `groups`. A program takes and returns all parts, laid end to end along the dimension named above; each array names one. Nothing has to cross between parts.
Inputs may be any that keep to these rules, and one draw needn't show every extreme that they name: `masked_bins`: distinct bins.
All inputs are finite; a program needn't handle non-finite values.
Results may differ from a plain program's by a relative error of at most 0.00083.
Values may be sent and summed in bfloat16 or wider, within the bound.
No kernel may reach another device: no remote copies, remote signals or barrier semaphores. Data moves between devices by JAX's collectives and lax.ppermute only.
A program may use at most 64 MiB of HBM per device.

v0:
```python
import jax
import jax.numpy as jnp
from jax import lax
from jax.sharding import PartitionSpec as P

WMAX = 3


def with_halo(cells, sides, width):
    for axis, dim in sides:
        count = lax.axis_size(axis)
        ends = count - 1
        head = lax.slice_in_dim(cells, 0, width, axis=dim)
        tail = lax.slice_in_dim(cells, cells.shape[dim] - width, cells.shape[dim], axis=dim)
        cells = jnp.concatenate(
            [
                lax.ppermute(tail, axis, [(i, (i + 1) % count) for i in range(ends)]),
                cells,
                lax.ppermute(head, axis, [((i + 1) % count, i) for i in range(ends)]),
            ],
            axis=dim,
        )
    return cells


def smooth(padded, radius_map):
    rows_here = padded.shape[0] - 2 * WMAX
    col_count = padded.shape[1] - 2 * WMAX
    row_sums = padded[WMAX : WMAX + rows_here]
    smoothed = jnp.zeros((rows_here, col_count), jnp.float32)
    for radius in range(WMAX + 1):
        if radius > 0:
            row_sums = (
                row_sums
                + padded[WMAX - radius : WMAX - radius + rows_here]
                + padded[WMAX + radius : WMAX + radius + rows_here]
            )
        box_sums = row_sums[:, WMAX : WMAX + col_count]
        for offset in range(1, radius + 1):
            box_sums = (
                box_sums
                + row_sums[:, WMAX - offset : WMAX - offset + col_count]
                + row_sums[:, WMAX + offset : WMAX + offset + col_count]
            )
        smoothed = smoothed + jnp.where(
            radius_map == radius, box_sums / float((2 * radius + 1) ** 2), 0.0
        )
    return smoothed


def pair_counts(first_bin, nrows, col_count):
    distance = jnp.arange(col_count, dtype=jnp.int32)
    upper_pairs = jnp.clip(col_count - distance - first_bin, 0, nrows)
    lower_pairs = jnp.clip(first_bin + nrows - distance, 0, nrows)
    pair_total = jnp.where(distance == 0, nrows, upper_pairs + lower_pairs)
    return jnp.maximum(pair_total, 1).astype(jnp.float32)


def mirrored_table(table):
    return jnp.concatenate([table[1:][::-1], table])


def skewed_map(table, window_first, rows_here, col_count):
    span = col_count + rows_here - 1
    window = lax.dynamic_slice_in_dim(mirrored_table(table), window_first, span)
    tiled = jnp.tile(window, rows_here + 1)[: rows_here * (span + 1)]
    shifted = tiled.reshape(rows_here, span + 1)[:, :col_count]
    return shifted[::-1]


def diagonal_totals(smoothed, window_first):
    rows_here = smoothed.shape[0]
    col_count = smoothed.shape[1]
    span = col_count + rows_here - 1
    flipped = jnp.pad(smoothed[::-1], ((0, 0), (0, rows_here)))
    flat = flipped.reshape(rows_here * (col_count + rows_here))[: rows_here * span]
    offsets = jnp.sum(flat.reshape(rows_here, span), axis=0)
    spread = lax.dynamic_update_slice_in_dim(
        jnp.zeros((2 * col_count - 1,), jnp.float32), offsets, window_first, 0
    )
    lower = jnp.concatenate([jnp.zeros((1,), jnp.float32), spread[: col_count - 1][::-1]])
    return spread[col_count - 1 :] + lower


def normalize(smoothed, expected_map, kept_rows, kept_cols):
    ratio = smoothed / expected_map
    kept_total = jnp.sum(kept_cols)
    row_mean = jnp.sum(ratio * kept_cols[None, :], axis=1, keepdims=True) / kept_total
    centred = (ratio - row_mean) * kept_cols[None, :]
    variance = jnp.sum(centred * centred, axis=1, keepdims=True) / kept_total
    zscores = (centred * lax.rsqrt(variance + 1e-05) * kept_rows[:, None]).astype(jnp.bfloat16)
    return (zscores, kept_total)


def cross_block(left, right):
    return lax.dot_general(
        left, right, (((1,), (1,)), ((), ())), preferred_element_type=jnp.float32
    )


def shards(contacts, widths, masked_bins, row_start):
    blocks = lax.axis_size("blk")
    position = lax.axis_index("blk")
    rows_here = contacts.shape[0]
    col_count = contacts.shape[1]
    nbins = rows_here * blocks
    first_row = position * rows_here
    first_bin = row_start[0]
    window_first = col_count - 1 - (first_bin + first_row + rows_here - 1)
    radius_map = skewed_map(widths, window_first, rows_here, col_count)
    padded_rows = with_halo(contacts, (("blk", 0),), WMAX)
    padded = jnp.pad(padded_rows, ((0, 0), (WMAX, WMAX)))
    smoothed = smooth(padded, radius_map)
    local_total = diagonal_totals(smoothed, window_first)
    denominator = pair_counts(first_bin, nbins, col_count)
    expected = lax.psum(local_total, "blk") / denominator
    expected_map = skewed_map(expected, window_first, rows_here, col_count)
    kept_bins = jnp.ones((col_count,), jnp.float32).at[masked_bins].set(0.0)
    kept_rows = lax.dynamic_slice_in_dim(kept_bins, first_bin + first_row, rows_here)
    zscores, kept_total = normalize(smoothed, expected_map, kept_rows, kept_bins)
    return cross_block(zscores, lax.all_gather(zscores, "blk", axis=0, tiled=True)) / kept_total


def solution(mesh):
    return jax.shard_map(
        shards,
        mesh=mesh,
        in_specs=(P(("groups", "blk"), None), P("groups"), P("groups"), P("groups")),
        out_specs=P(("groups", "blk"), None),
        check_vma=False,
    )
```

profile of v0, /device:TPU:0, one launch (start us, length us, event | category | flops | bytes accessed | tf_op | source)
XLA Modules:
  0.0 145.9 jit_solution(1816043342483909816)
XLA Ops:
  6.5 1.1 fusion.14
  7.6 2.4 %collective-permute-start = (f32[3,6144]{1,0:T(4,128)S(1)}, f32[3,6144]{1,0:T(4,128)S(1)}, u32[]{:S(2)}, u32[]{:S(2)}) collective-permute-start(f32[3,6144]{1,0:T(4,128)S(1)} %get-tuple-element.10), channel_id=1, source_target_pairs={{0,1},{1,2},{2,3},{3,4},{4,5},{5,6},{6,7},{7,8},{8,9},{9,10},{10,1... | collective-permute-start | bytes 221192 | tf_op jit(solution)/shard_map/ppermute | solution.py:17
  10.1 1.3 collective-permute-start.1
  12.0 0.7 compare_select_fusion
  12.7 2.9 %scatter_custom_fusion = f32[6144]{0:T(1024)S(1)} fusion(s32[384]{0:T(512)S(1)} %compare_select_fusion, f32[384]{0:T(512)S(1)} %broadcast.30, f32[]{:T(128)} %constant.14.clone.1), kind=kCustom, calls=%fused_computation.47 | custom fusion | bytes 24580 | tf_op jit(solution)/shard_map/scatter | solution.py:118
  15.7 0.7 reduce_sum.38
  16.4 0.8 slice.102
  17.4 0.8 fusion.11
  18.8 0.8 rev.19
  19.6 0.3 select_maximum_fusion
  19.9 0.2 slice_add_fusion
  20.2 1.5 %fusion.3 = f32[16,6144]{1,0:T(8,128)S(1)} fusion(f32[16,6150]{1,0:T(8,128)S(1)} %get-tuple-element.7, f32[16,6150]{1,0:T(8,128)S(1)} %get-tuple-element.8, f32[16,6150]{1,0:T(8,128)S(1)} %get-tuple-element.9, f32[16,6144]{1,0:T(8,128)S(1)} %copy-done, s32[16,6144]{1,0:T(8,128)S(1)} %rev.19), kind=kLoop, calls=%fused_computation.16 | loop fusion | flops 2555904 | bytes 7077888 | tf_op jit(solution)/shard_map/add | solution.py:45
  21.7 0.8 rev.20
  22.5 0.3 reshape.29
  22.8 0.3 reshape.30
  23.1 0.5 dynamic_update_slice.3
  23.9 63.8 %psum.7 = f32[6144]{0:T(1024)S(1)} all-reduce(f32[6144]{0:T(1024)S(1)} %slice_add_fusion.18), channel_id=1, replica_groups=mesh['groups'=2,'blk'=16] {'blk'}, use_global_device_ids=true, to_apply=%region_1.2 | all-reduce | flops 6144 | bytes 49152 | tf_op jit(solution)/shard_map/psum | solution.py:116
  88.7 0.8 rev.23
  89.7 0.6 broadcast_divide_fusion
  90.3 0.3 multiply_reduce_fusion
  90.6 0.6 add_rsqrt_fusion
  91.2 0.8 multiply_convert_fusion
  92.1 42.8 %all-gather.2.cloned.1.call-done = bf16[256,6144]{1,0:T(8,128)(2,1)} async-done(((bf16[16,6144]{1,0:T(8,128)(2,1)}), bf16[256,6144]{1,0:T(8,128)(2,1)}) %all-gather.2.cloned.1.call-update) | async-done | bytes 3145744 | tf_op jit(solution)/shard_map/all_gather | solution.py:121
  134.9 4.2 %convolution_divide_fusion = f32[16,256]{1,0:T(8,128)} fusion(bf16[16,6144]{1,0:T(8,128)(2,1)} %multiply_convert_fusion, bf16[256,6144]{1,0:T(8,128)(2,1)} %all-gather.2.cloned.1.call-done, f32[]{:T(128)} %reduce_sum.38), kind=kOutput, calls=%fused_computation.1 | convolution fusion | flops 50335744 | bytes 3358724 | tf_op jit(solution)/shard_map/dot_general | solution.py:96
  (33 shorter events, 2.3 us)
Async XLA Ops:
  6.5 13.1 %copy-start = (f32[16,6144]{1,0:T(8,128)S(1)}, f32[16,6144]{1,0:T(8,128)}, u32[]{:S(2)}) copy-start(f32[16,6144]{1,0:T(8,128)} %param.4) | copy-start | bytes 1179652
  6.5 128.4 %all-gather.2.cloned.1.call-start = ((), (), s32[]{:S(2)}) async-start(), calls=%async_computation | async-start | bytes 3342336 | tf_op jit(solution)/shard_map/all_gather | solution.py:121
  7.6 11.9 %collective-permute-start = (f32[3,6144]{1,0:T(4,128)S(1)}, f32[3,6144]{1,0:T(4,128)S(1)}, u32[]{:S(2)}, u32[]{:S(2)}) collective-permute-start(f32[3,6144]{1,0:T(4,128)S(1)} %get-tuple-element.10), channel_id=1, source_target_pairs={{0,1},{1,2},{2,3},{3,4},{4,5},{5,6},{6,7},{7,8},{8,9},{9,10},{10,1... | collective-permute-start | bytes 221192 | tf_op jit(solution)/shard_map/ppermute | solution.py:17
  10.1 9.5 %collective-permute-start.1 = (f32[3,6144]{1,0:T(4,128)S(1)}, f32[3,6144]{1,0:T(4,128)S(1)}, u32[]{:S(2)}, u32[]{:S(2)}) collective-permute-start(f32[3,6144]{1,0:T(4,128)S(1)} %get-tuple-element.11), channel_id=1, source_target_pairs={{1,0},{2,1},{3,2},{4,3},{5,4},{6,5},{7,6},{8,7},{9,8},{10,9},{11,1... | collective-permute-start | bytes 221192 | tf_op jit(solution)/shard_map/ppermute | solution.py:19
Sparse Core Ops, SparseCore 0:
  92.2 42.6 all-gather.1
where the time goes:
time: 146 us
  blocking collectives  63.8 us (44%)
  waiting for transfers between devices  42.9 us (29%)
  between operations  14.3 us (10%)
  local copies, waits for them, and re-layouts  10 us (7%)
  other arithmetic  7.05 us (5%)
  matrix products  4.17 us (3%)
  starting transfers between devices  3.7 us (3%)
    psum x1, blocking collectives, shards(): expected = lax.psum(local_total, 'blk') / denominator  63.8 us
    all_gather x1, waiting for transfers between devices, shards(): lax.all_gather(zscores, 'blk', axis=0, tiled=True)  42.8 us
    dot_general x1, matrix products, cross_block(): lax.dot_general(left, right, (((1,), (1,)), ((), ())), preferred_element_...  4.17 us
    scatter x1, local copies, waits for them, and re-layouts, shards(): kept_bins = jnp.ones((col_count,), jnp.float32).at[masked_bins].set(0.0)  2.95 us
  transfers between devices with their start and end apart: 3, of which 1 were waited for; matrix products, arithmetic and copies ran while one was open for 5% of the time, Pallas kernels for 0%

commit v1 on v0

--- a/solution.py
+++ b/solution.py
@@ -4,6 +4,18 @@
 from jax.sharding import PartitionSpec as P
 
 WMAX = 3
+
+
+def collect(shard, axis, dim):
+    ways, here, turn = (lax.axis_size(axis), lax.axis_index(axis), shard.shape[dim])
+    line, have = (shard, 1)
+    while have < ways:
+        line = jnp.concatenate(
+            [line, lax.ppermute(line, axis, [(d, (d - have) % ways) for d in range(ways)])],
+            axis=dim,
+        )
+        have = 2 * have
+    return jnp.roll(line, here * turn, axis=dim)
 
 
 def with_halo(cells, sides, width):
@@ -118,7 +130,7 @@
     kept_bins = jnp.ones((col_count,), jnp.float32).at[masked_bins].set(0.0)
     kept_rows = lax.dynamic_slice_in_dim(kept_bins, first_bin + first_row, rows_here)
     zscores, kept_total = normalize(smoothed, expected_map, kept_rows, kept_bins)
-    return cross_block(zscores, lax.all_gather(zscores, "blk", axis=0, tiled=True)) / kept_total
+    return cross_block(zscores, collect(zscores, "blk", 0)) / kept_total
 
 
 def solution(mesh):

time: 146 us -> 199 us (1.36)
  waiting for transfers between devices: 42.9 us -> 100 us
  between operations: 14.3 us -> 0.99 us
  local copies, waits for them, and re-layouts: 10 us -> 18.1 us
    ppermute x0 -> x4, waiting for transfers between devices: none -> 100 us  [collect(): lax.ppermute(line, axis, [(d, (d - have) % ways) for d in range(ways)])]
    all_gather x1 -> x0, waiting for transfers between devices: 42.8 us -> none  [shards(): lax.all_gather(zscores, 'blk', axis=0, tiled=True)]
    unnamed x8 -> x16, local copies, waits for them, and re-layouts: 0.47 us -> 7.23 us
  transfers between devices with their start and end apart: 3 -> 6, of which waited for: 1 -> 4; matrix products, arithmetic and copies ran while one was open for 5% -> 5% of each run, Pallas kernels for 0% -> 0%
where the time goes in v1:
time: 199 us
  waiting for transfers between devices  100 us (50%)
  blocking collectives  63.8 us (32%)
  local copies, waits for them, and re-layouts  18.1 us (9%)
  other arithmetic  8.05 us (4%)
  matrix products  4 us (2%)
  starting transfers between devices  3.88 us (2%)
    ppermute x4, waiting for transfers between devices, collect(): lax.ppermute(line, axis, [(d, (d - have) % ways) for d in range(ways)])  100 us
    psum x1, blocking collectives, shards(): expected = lax.psum(local_total, 'blk') / denominator  63.8 us
    unnamed x16, local copies, waits for them, and re-layouts  7.23 us
    dot_general x1, matrix products, cross_block(): lax.dot_general(left, right, (((1,), (1,)), ((), ())), preferred_element_...  4 us
  transfers between devices with their start and end apart: 6, of which 4 were waited for; matrix products, arithmetic and copies ran while one was open for 5% of the time, Pallas kernels for 0%

profile of v1, /device:TPU:0, one launch (start us, length us, event | category | flops | bytes accessed | tf_op | source)
XLA Modules:
  0.0 198.8 jit_solution(1254043987764885319)
XLA Ops:
  0.0 1.1 fusion.20
  1.1 2.4 %collective-permute-start = (f32[3,6144]{1,0:T(4,128)S(1)}, f32[3,6144]{1,0:T(4,128)S(1)}, u32[]{:S(2)}, u32[]{:S(2)}) collective-permute-start(f32[3,6144]{1,0:T(4,128)S(1)} %get-tuple-element.12), channel_id=1, source_target_pairs={{0,1},{1,2},{2,3},{3,4},{4,5},{5,6},{6,7},{7,8},{8,9},{9,10},{10,1... | collective-permute-start | bytes 221192 | tf_op jit(solution)/shard_map/ppermute | solution.py:29
  3.5 1.3 collective-permute-start.1
  6.2 2.9 %scatter_custom_fusion = f32[6144]{0:T(1024)S(1)} fusion(s32[384]{0:T(512)S(1)} %compare_select_fusion, f32[384]{0:T(512)S(1)} %broadcast.31, f32[]{:T(128)} %constant.70.clone.1), kind=kCustom, calls=%fused_computation.62 | custom fusion | bytes 24580 | tf_op jit(solution)/shard_map/scatter | solution.py:130
  9.8 0.8 slice.102
  10.8 0.8 fusion.16
  12.2 0.8 rev.19
  13.0 1.3 select_maximum_fusion
  14.6 1.5 fusion.8
  16.1 0.8 rev.20
  18.3 63.8 %psum.7 = f32[6144]{0:T(1024)S(1)} all-reduce(f32[6144]{0:T(1024)S(1)} %slice_add_fusion.18), channel_id=1, replica_groups=mesh['groups'=2,'blk'=16] {'blk'}, use_global_device_ids=true, to_apply=%region_1.2 | all-reduce | flops 6144 | bytes 49152 | tf_op jit(solution)/shard_map/psum | solution.py:128
  83.1 0.8 rev.23
  85.5 0.8 constant_dynamic-update-slice_fusion.9
  86.3 3.2 %collective-permute-done.2 = bf16[16,6144]{1,0:T(8,128)(2,1)S(1)} collective-permute-done((bf16[16,6144]{1,0:T(8,128)(2,1)S(1)}, bf16[16,6144]{1,0:T(8,128)(2,1)S(1)}, u32[]{:S(2)}, u32[]{:S(2)}) %collective-permute-start.2) | collective-permute-done | bytes 196640 | tf_op jit(solution)/shard_map/ppermute | solution.py:14
  89.6 9.4 %collective-permute-done.3 = bf16[32,6144]{1,0:T(8,128)(2,1)S(1)} collective-permute-done((bf16[32,6144]{1,0:T(8,128)(2,1)S(1)}, bf16[32,6144]{1,0:T(8,128)(2,1)S(1)}, u32[]{:S(2)}, u32[]{:S(2)}) %collective-permute-start.3) | collective-permute-done | bytes 393248 | tf_op jit(solution)/shard_map/ppermute | solution.py:14
  99.1 19.6 %collective-permute-done.4 = bf16[64,6144]{1,0:T(8,128)(2,1)S(1)} collective-permute-done((bf16[64,6144]{1,0:T(8,128)(2,1)S(1)}, bf16[64,6144]{1,0:T(8,128)(2,1)S(1)}, u32[]{:S(2)}, u32[]{:S(2)}) %collective-permute-start.4) | collective-permute-done | bytes 786464 | tf_op jit(solution)/shard_map/ppermute | solution.py:14
  119.7 0.8 constant_dynamic-update-slice_fusion.7
  120.4 1.0 constant_dynamic-update-slice_fusion.6
  121.4 67.8 %collective-permute-done.5 = bf16[128,6144]{1,0:T(8,128)(2,1)S(1)} collective-permute-done((bf16[128,6144]{1,0:T(8,128)(2,1)S(1)}, bf16[128,6144]{1,0:T(8,128)(2,1)S(1)}, u32[]{:S(2)}, u32[]{:S(2)}) %collective-permute-start.5) | collective-permute-done | bytes 1572896 | tf_op jit(solution)/shard_map/ppermute | solution.py:14
  189.2 1.3 constant_dynamic-update-slice_fusion.5
  191.9 0.8 constant_dynamic-update-slice_fusion.2
  192.6 0.9 constant_dynamic-update-slice_fusion.1
  193.6 1.3 constant_dynamic-update-slice_fusion
  194.8 4.0 %fusion.2 = f32[16,256]{1,0:T(8,128)} fusion(bf16[16,6144]{1,0:T(8,128)(2,1)S(1)} %get-tuple-element.6, bf16[512,6144]{1,0:T(8,128)(2,1)} %constant_dynamic-update-slice_fusion, s32[]{:T(128)S(6)} %select_n.50, f32[]{:T(128)} %reduce_sum.38), kind=kOutput, calls=%fused_computation.4 | convolution fusion | flops 50335744 | bytes 3359236 | tf_op jit(solution)/shard_map/dot_general | solution.py:108
  (50 shorter events, 8.7 us)
Async XLA Ops:
  0.0 14.6 %copy-start = (f32[16,6144]{1,0:T(8,128)S(1)}, f32[16,6144]{1,0:T(8,128)}, u32[]{:S(2)}) copy-start(f32[16,6144]{1,0:T(8,128)} %param.4) | copy-start | bytes 1179652
  1.1 11.9 %collective-permute-start = (f32[3,6144]{1,0:T(4,128)S(1)}, f32[3,6144]{1,0:T(4,128)S(1)}, u32[]{:S(2)}, u32[]{:S(2)}) collective-permute-start(f32[3,6144]{1,0:T(4,128)S(1)} %get-tuple-element.12), channel_id=1, source_target_pairs={{0,1},{1,2},{2,3},{3,4},{4,5},{5,6},{6,7},{7,8},{8,9},{9,10},{10,1... | collective-permute-start | bytes 221192 | tf_op jit(solution)/shard_map/ppermute | solution.py:29
  3.5 9.5 %collective-permute-start.1 = (f32[3,6144]{1,0:T(4,128)S(1)}, f32[3,6144]{1,0:T(4,128)S(1)}, u32[]{:S(2)}, u32[]{:S(2)}) collective-permute-start(f32[3,6144]{1,0:T(4,128)S(1)} %get-tuple-element.13), channel_id=1, source_target_pairs={{1,0},{2,1},{3,2},{4,3},{5,4},{6,5},{7,6},{8,7},{9,8},{10,9},{11,1... | collective-permute-start | bytes 221192 | tf_op jit(solution)/shard_map/ppermute | solution.py:31
  86.3 3.2 %collective-permute-start.2 = (bf16[16,6144]{1,0:T(8,128)(2,1)S(1)}, bf16[16,6144]{1,0:T(8,128)(2,1)S(1)}, u32[]{:S(2)}, u32[]{:S(2)}) collective-permute-start(bf16[16,6144]{1,0:T(8,128)(2,1)S(1)} %get-tuple-element.6), channel_id=1, source_target_pairs={{0,15},{1,0},{2,1},{3,2},{4,3},{5,4},{6,5},{7,6},{8,7},{9,8},{10,9... | collective-permute-start | bytes 589832 | tf_op jit(solution)/shard_map/ppermute | solution.py:14
  89.5 9.5 %collective-permute-start.3 = (bf16[32,6144]{1,0:T(8,128)(2,1)S(1)}, bf16[32,6144]{1,0:T(8,128)(2,1)S(1)}, u32[]{:S(2)}, u32[]{:S(2)}) collective-permute-start(bf16[32,6144]{1,0:T(8,128)(2,1)S(1)} %pad_maximum_fusion.2), channel_id=1, source_target_pairs={{0,14},{1,15},{2,0},{3,1},{4,2},{5,3},{6,4},{7,5},{8,6},{9,7},{10,... | collective-permute-start | bytes 1179656 | tf_op jit(solution)/shard_map/ppermute | solution.py:14
  99.1 19.7 %collective-permute-start.4 = (bf16[64,6144]{1,0:T(8,128)(2,1)S(1)}, bf16[64,6144]{1,0:T(8,128)(2,1)S(1)}, u32[]{:S(2)}, u32[]{:S(2)}) collective-permute-start(bf16[64,6144]{1,0:T(8,128)(2,1)S(1)} %pad_maximum_fusion.1), channel_id=1, source_target_pairs={{0,12},{1,13},{2,14},{3,15},{4,0},{5,1},{6,2},{7,3},{8,4},{9,5},{1... | collective-permute-start | bytes 2359304 | tf_op jit(solution)/shard_map/ppermute | solution.py:14
  118.9 70.3 %collective-permute-start.5 = (bf16[128,6144]{1,0:T(8,128)(2,1)S(1)}, bf16[128,6144]{1,0:T(8,128)(2,1)S(1)}, u32[]{:S(2)}, u32[]{:S(2)}) collective-permute-start(bf16[128,6144]{1,0:T(8,128)(2,1)S(1)} %pad_maximum_fusion), channel_id=1, source_target_pairs={{0,8},{1,9},{2,10},{3,11},{4,12},{5,13},{6,14},{7,15},{8,0},{9,1},... | collective-permute-start | bytes 4718600 | tf_op jit(solution)/shard_map/ppermute | solution.py:14
